TPU v7x, 32 devices: a whole 2x2x4 slice. The times are simulated.
32 devices in a mesh: grp: 2 (over x), date: 16 (over z, y, core).
Axes of the slice: x: 2, y: 2, z: 4, core: 2. Of those that a mesh axis runs over, the one named last changes fastest.
Arguments:
- slc: bfloat16 [16, 2, 128, 2048], P('date', None, 'grp'), parts along dimension 2, may hold values from -6 to 6
- pairs: int32 [64, 2], replicated, may hold values from 0 to 15, as said below
- inverse: bfloat16 [15, 64], replicated, may hold values from -6 to 6
Outputs:
- series: float32 [15, 32, 128], P(None, ('grp', 'date')), parts along dimension 1
There are 2 independent parts, one for each index of `grp`. A program takes and returns all parts, laid end to end along the dimension named above; an argument that names none is the same for every part. Nothing has to cross between parts.
Inputs may be any that keep to these rules, and one draw needn't show every extreme that they name: pairs[p,0] < pairs[p,1] for every pair.
All inputs are finite; a program needn't handle non-finite values.
Results may differ from a plain program's by a relative error of at most 0.0003.
Values may be sent and summed in bfloat16 or wider, within the bound.
No kernel may reach another device: no remote copies, remote signals or barrier semaphores. Data moves between devices by JAX's collectives and lax.ppermute only.
A program may use at most 128 MiB of HBM per device.

v0:
```python
import jax
import jax.numpy as jnp
from jax import lax
from jax.sharding import PartitionSpec as P

LOOK_R = 4
LOOK_C = 16


def coherence(first, second):
    first = first.astype(jnp.float32)
    second = second.astype(jnp.float32)
    cross = first[:, 1] * second[:, 0] - first[:, 0] * second[:, 1]
    power_ref = first[:, 0] * first[:, 0] + first[:, 1] * first[:, 1]
    power_sec = second[:, 0] * second[:, 0] + second[:, 1] * second[:, 1]
    stacked = jnp.stack([cross, power_ref, power_sec])
    three, count, rows, cols = stacked.shape
    rowsum = stacked.reshape(three, count, rows // LOOK_R, LOOK_R, cols).sum(axis=3)
    window = (jnp.arange(cols)[:, None] // LOOK_C == jnp.arange(cols // LOOK_C)[None, :]).astype(
        jnp.float32
    )
    looked = jnp.dot(rowsum, window, precision=lax.Precision.HIGHEST)
    return looked[0] / jnp.sqrt(looked[1] * looked[2] + 1e-06)


def invert(inverse, proxy):
    return jnp.einsum(
        "sp,pxy->sxy", inverse.astype(jnp.float32), proxy, precision=lax.Precision.HIGHEST
    )


def per_device(slc, pairs, inverse):
    stripes = lax.all_to_all(slc, "date", split_axis=2, concat_axis=0, tiled=True)
    first = jnp.take(stripes, pairs[:, 0], axis=0)
    second = jnp.take(stripes, pairs[:, 1], axis=0)
    proxy = coherence(first, second)
    return invert(inverse, proxy)


def solution(mesh):
    in_specs = (P("date", None, "grp", None), P(), P())
    out_specs = P(None, ("grp", "date"), None)
    return jax.shard_map(
        per_device, mesh=mesh, in_specs=in_specs, out_specs=out_specs, check_vma=False
    )
```

profile of v0, /device:TPU:0, one launch (start us, length us, event | category | flops | bytes accessed | tf_op | source)
XLA Modules:
  0.0 41.9 jit_solution(5127418015980830979)
XLA Ops:
  0.0 0.0 copy-start
  0.0 0.0 copy-start.1
  0.0 2.4 %copy.26 = bf16[1,2,64,2048]{3,1,0,2:T(2,128)(2,1)} copy(bf16[1,2,64,2048]{3,2,1,0:T(8,128)(2,1)} %param.5) | data formatting | bytes 1048576 | tf_op args[0]
  2.4 7.4 %all-to-all-start = ((bf16[1,2,64,2048]{3,1,0,2:T(2,128)(2,1)}), bf16[1,2,64,2048]{3,1,0,2:T(2,128)(2,1)S(1)}, u32[]{:S(2)}, u32[]{:S(2)}) async-start(bf16[1,2,64,2048]{3,1,0,2:T(2,128)(2,1)} %copy.26), calls=%async_computation | async-start | bytes 1048576 | tf_op jit(solution)/shard_map/all_to_all | solution.py:33
  9.8 0.0 copy-done.1
  9.9 14.2 %all-to-all-done = bf16[1,2,64,2048]{3,1,0,2:T(2,128)(2,1)S(1)} async-done(((bf16[1,2,64,2048]{3,1,0,2:T(2,128)(2,1)}), bf16[1,2,64,2048]{3,1,0,2:T(2,128)(2,1)S(1)}, u32[]{:S(2)}, u32[]{:S(2)}) %all-to-all-start) | async-done | bytes 524320 | tf_op jit(solution)/shard_map/all_to_all | solution.py:33
  24.1 0.3 copy.38
  24.4 2.4 %gather_fusion = bf16[64,2,4,2048]{3,2,1,0:T(4,128)(2,1)S(1)} fusion(bf16[16,2,4,2048]{3,2,1,0:T(4,128)(2,1)S(1)} %bitcast.30, s32[1024]{0:T(1024)S(1)} %pad_clamp_fusion.1), kind=kCustom, calls=%fused_computation.clone | custom fusion | bytes 4194560 | tf_op jit(solution)/shard_map/jit(_take)/gather | solution.py:34
  26.7 3.6 %gather_fusion.1 = bf16[64,2,4,2048]{3,2,1,0:T(4,128)(2,1)} fusion(bf16[16,2,4,2048]{3,2,1,0:T(4,128)(2,1)S(1)} %bitcast.31, s32[1024]{0:T(1024)S(1)} %pad_clamp_fusion), kind=kCustom, calls=%fused_computation.1.clone | custom fusion | bytes 4194560 | tf_op jit(solution)/shard_map/jit(_take)/gather | solution.py:35
  30.3 7.5 %fusion = (f32[64,2,4,2048]{3,0,2,1:T(8,128)S(1)}, f32[64,2,4,2048]{3,0,2,1:T(8,128)S(1)}) fusion(bf16[64,2,4,2048]{3,2,1,0:T(4,128)(2,1)} %gather_fusion.1, pred[64]{0:T(512)(128)(4,1)S(1)} %get-tuple-element.13, bf16[64,2,4,2048]{3,2,1,0:T(4,128)(2,1)S(1)} %gather_fusion, pred[64]{0:T(512)(128)(4,1)S(1)} %get-tuple-element.6), kind=kLoop, calls=%fused_computation.4 | loop fusion | flops 4194304 | bytes 12583040 | tf_op jit(solution)/shard_map/convert_element_type | solution.py:12
  37.8 1.6 %subtract_bitcast_fusion = (f32[1,64,4,2048]{3,1,2,0:T(8,128)S(1)}, f32[1,64,4,2048]{3,1,2,0:T(8,128)S(1)}, f32[1,64,4,2048]{3,1,2,0:T(8,128)S(1)}) fusion(f32[64,2,4,2048]{3,0,2,1:T(8,128)S(1)} %get-tuple-element.15, f32[64,2,4,2048]{3,0,2,1:T(8,128)S(1)} %get-tuple-element.16), kind=kLoop, calls=%fused_computation.9 | loop fusion | flops 4718592 | bytes 14680064 | tf_op jit(solution)/shard_map/sub | solution.py:13
  39.5 0.7 %maximum_reduce_fusion = f32[3,64,2048]{2,1,0:T(8,128)S(1)} fusion(f32[1,64,4,2048]{3,1,2,0:T(8,128)S(1)} %get-tuple-element.12, f32[1,64,4,2048]{3,1,2,0:T(8,128)S(1)} %get-tuple-element.11, f32[1,64,4,2048]{3,1,2,0:T(8,128)S(1)} %get-tuple-element.10), kind=kLoop, calls=%fused_computation.2 | loop fusion | flops 4325376 | bytes 7864320 | tf_op jit(solution)/shard_map/reduce_sum | solution.py:18
  40.1 1.0 %fusion.3 = f32[3,64,128]{2,1,0:T(8,128)S(1)} fusion(f32[3,64,2048]{2,1,0:T(8,128)S(1)} %maximum_reduce_fusion, s32[2048]{0:T(1024)S(1)} %add_select_fusion), kind=kOutput, calls=%fused_computation.13 | convolution fusion | flops 604241920 | bytes 1679360 | tf_op jit(solution)/shard_map/dot_general | solution.py:22
  41.2 0.0 copy-done
  41.2 0.1 convolution_bitcast_fusion
  41.3 0.6 %copy.30 = f32[15,1,128]{2,1,0:T(1,128)} copy(f32[15,1,128]{2,0,1:T(8,128)S(1)} %convolution_bitcast_fusion) | data formatting | bytes 15360 | tf_op jit(solution)/shard_map/sp,pxy->sxy/dot_general | solution.py:27
  (4 shorter events, 0.0 us)
Async XLA Ops:
  0.0 41.2 %copy-start = (bf16[15,64]{1,0:T(8,128)(2,1)S(1)}, bf16[15,64]{1,0:T(8,128)(2,1)}, u32[]{:S(2)}) copy-start(bf16[15,64]{1,0:T(8,128)(2,1)} %param.7) | copy-start | bytes 5764
  0.0 9.8 %copy-start.1 = (s32[64,2]{0,1:T(2,128)S(1)}, s32[64,2]{0,1:T(2,128)}, u32[]{:S(2)}) copy-start(s32[64,2]{0,1:T(2,128)} %param.6) | copy-start | bytes 1540
  2.4 21.7 %all-to-all-start = ((bf16[1,2,64,2048]{3,1,0,2:T(2,128)(2,1)}), bf16[1,2,64,2048]{3,1,0,2:T(2,128)(2,1)S(1)}, u32[]{:S(2)}, u32[]{:S(2)}) async-start(bf16[1,2,64,2048]{3,1,0,2:T(2,128)(2,1)} %copy.26), calls=%async_computation | async-start | bytes 1048576 | tf_op jit(solution)/shard_map/all_to_all | solution.py:33
where the time goes:
time: 42.2 us; the launch traced here: 41.9 us
  waiting for transfers between devices  14.2 us (34%)
  other arithmetic  9.83 us (23%)
  local copies, waits for them, and re-layouts  9.23 us (22%)
  starting transfers between devices  7.41 us (18%)
  matrix products  1.16 us (3%)
    all_to_all x1, waiting for transfers between devices, per_device(): lax.all_to_all(slc, 'date', split_axis=2, concat_axis=0, tiled=True)  14.2 us
    convert_element_type x1, other arithmetic, coherence(): second = second.astype(jnp.float32)  7.53 us
    all_to_all x1, starting transfers between devices, per_device(): lax.all_to_all(slc, 'date', split_axis=2, concat_axis=0, tiled=True)  7.41 us
    gather x1, local copies, waits for them, and re-layouts, per_device(): second = jnp.take(stripes, pairs[:, 1], axis=0)  3.56 us
    unnamed x5, local copies, waits for them, and re-layouts  2.41 us
    gather x1, local copies, waits for them, and re-layouts, per_device(): first = jnp.take(stripes, pairs[:, 0], axis=0)  2.36 us
    sub x1, other arithmetic, coherence(): cross = first[:, 1] * second[:, 0] - first[:, 0] * second[:, 1]  1.62 us
    dot_general x1, matrix products, coherence(): looked = jnp.dot(rowsum, window, precision=lax.Precision.HIGHEST)  1.03 us
  transfers between devices with their start and end apart: 1, of which 1 were waited for; matrix products, arithmetic and copies ran while one was open for 0% of the time, Pallas kernels for 0%

commit v1 on v0

--- a/solution.py
+++ b/solution.py
@@ -30,7 +30,10 @@
 
 
 def per_device(slc, pairs, inverse):
-    stripes = lax.all_to_all(slc, "date", split_axis=2, concat_axis=0, tiled=True)
+    devices = lax.axis_size("date")
+    tiles = jnp.stack(jnp.split(slc, devices, axis=2), axis=0)
+    tiles = lax.all_to_all(tiles, "date", split_axis=0, concat_axis=0)
+    stripes = jnp.concatenate(tiles, axis=0)
     first = jnp.take(stripes, pairs[:, 0], axis=0)
     second = jnp.take(stripes, pairs[:, 1], axis=0)
     proxy = coherence(first, second)

time: 42.2 us -> 63.7 us (1.51); the launches traced: 41.9 us -> 62.7 us
  local copies, waits for them, and re-layouts: 9.23 us -> 30 us
    unnamed x5 -> x19, local copies, waits for them, and re-layouts: 2.41 us -> 22 us
    another operation x0 -> x1, local copies, waits for them, and re-layouts: none -> 1.47 us  [per_device(): tiles = jnp.stack(jnp.split(slc, devices, axis=2), axis=0)]
where the time goes in v1:
time: 63.7 us; the launch traced here: 62.7 us
  local copies, waits for them, and re-layouts  30 us (47%)
  waiting for transfers between devices  14.2 us (22%)
  other arithmetic  9.83 us (15%)
  starting transfers between devices  7.41 us (12%)
  matrix products  1.16 us (2%)
    unnamed x19, local copies, waits for them, and re-layouts  22 us
    all_to_all x1, waiting for transfers between devices, per_device(): tiles = lax.all_to_all(tiles, 'date', split_axis=0, concat_axis=0)  14.2 us
    convert_element_type x1, other arithmetic, coherence(): second = second.astype(jnp.float32)  7.53 us
    all_to_all x1, starting transfers between devices, per_device(): tiles = lax.all_to_all(tiles, 'date', split_axis=0, concat_axis=0)  7.41 us
    gather x1, local copies, waits for them, and re-layouts, per_device(): second = jnp.take(stripes, pairs[:, 1], axis=0)  3.56 us
    gather x1, local copies, waits for them, and re-layouts, per_device(): first = jnp.take(stripes, pairs[:, 0], axis=0)  2.36 us
    sub x1, other arithmetic, coherence(): cross = first[:, 1] * second[:, 0] - first[:, 0] * second[:, 1]  1.62 us
    another operation x1, local copies, waits for them, and re-layouts, per_device(): tiles = jnp.stack(jnp.split(slc, devices, axis=2), axis=0)  1.47 us
  transfers between devices with their start and end apart: 1, of which 1 were waited for; matrix products, arithmetic and copies ran while one was open for 0% of the time, Pallas kernels for 0%

profile of v1, /device:TPU:0, one launch (start us, length us, event | category | flops | bytes accessed | tf_op | source)
XLA Modules:
  0.0 62.7 jit_solution(13579332644770532090)
XLA Ops:
  0.0 0.0 copy-start
  0.0 0.0 copy-start.1
  0.0 1.5 %constant_dynamic-update-slice_fusion.15 = bf16[16,1,2,4,2048]{4,3,2,1,0:T(4,128)(2,1)} fusion(bf16[1,2,64,2048]{3,2,1,0:T(8,128)(2,1)} %param.5), kind=kLoop, calls=%fused_computation.37 | loop fusion | bytes 65536
  1.5 1.5 %constant_dynamic-update-slice_fusion.14 = bf16[16,1,2,4,2048]{4,3,2,1,0:T(4,128)(2,1)} fusion(bf16[16,1,2,4,2048]{4,3,2,1,0:T(4,128)(2,1)} %constant_dynamic-update-slice_fusion.15, bf16[1,2,64,2048]{3,2,1,0:T(8,128)(2,1)} %param.5), kind=kLoop, calls=%fused_computation.36 | loop fusion | bytes 65536
  3.0 1.5 %constant_dynamic-update-slice_fusion.13 = bf16[16,1,2,4,2048]{4,3,2,1,0:T(4,128)(2,1)} fusion(bf16[16,1,2,4,2048]{4,3,2,1,0:T(4,128)(2,1)} %constant_dynamic-update-slice_fusion.14, bf16[1,2,64,2048]{3,2,1,0:T(8,128)(2,1)} %param.5), kind=kLoop, calls=%fused_computation.35 | loop fusion | bytes 65536
  4.4 1.5 %constant_dynamic-update-slice_fusion.12 = bf16[16,1,2,4,2048]{4,3,2,1,0:T(4,128)(2,1)} fusion(bf16[16,1,2,4,2048]{4,3,2,1,0:T(4,128)(2,1)} %constant_dynamic-update-slice_fusion.13, bf16[1,2,64,2048]{3,2,1,0:T(8,128)(2,1)} %param.5), kind=kLoop, calls=%fused_computation.34 | loop fusion | bytes 65536
  5.9 1.5 %constant_dynamic-update-slice_fusion.11 = bf16[16,1,2,4,2048]{4,3,2,1,0:T(4,128)(2,1)} fusion(bf16[16,1,2,4,2048]{4,3,2,1,0:T(4,128)(2,1)} %constant_dynamic-update-slice_fusion.12, bf16[1,2,64,2048]{3,2,1,0:T(8,128)(2,1)} %param.5), kind=kLoop, calls=%fused_computation.33 | loop fusion | bytes 65536
  7.3 1.5 %constant_dynamic-update-slice_fusion.10 = bf16[16,1,2,4,2048]{4,3,2,1,0:T(4,128)(2,1)} fusion(bf16[16,1,2,4,2048]{4,3,2,1,0:T(4,128)(2,1)} %constant_dynamic-update-slice_fusion.11, bf16[1,2,64,2048]{3,2,1,0:T(8,128)(2,1)} %param.5), kind=kLoop, calls=%fused_computation.32 | loop fusion | bytes 65536
  8.8 1.5 %constant_dynamic-update-slice_fusion.9 = bf16[16,1,2,4,2048]{4,3,2,1,0:T(4,128)(2,1)} fusion(bf16[16,1,2,4,2048]{4,3,2,1,0:T(4,128)(2,1)} %constant_dynamic-update-slice_fusion.10, bf16[1,2,64,2048]{3,2,1,0:T(8,128)(2,1)} %param.5), kind=kLoop, calls=%fused_computation.31 | loop fusion | bytes 65536
  10.3 1.5 %constant_dynamic-update-slice_fusion.8 = bf16[16,1,2,4,2048]{4,3,2,1,0:T(4,128)(2,1)} fusion(bf16[16,1,2,4,2048]{4,3,2,1,0:T(4,128)(2,1)} %constant_dynamic-update-slice_fusion.9, bf16[1,2,64,2048]{3,2,1,0:T(8,128)(2,1)} %param.5), kind=kLoop, calls=%fused_computation.30 | loop fusion | bytes 65536
  11.7 1.5 %constant_dynamic-update-slice_fusion.7 = bf16[16,1,2,4,2048]{4,3,2,1,0:T(4,128)(2,1)} fusion(bf16[16,1,2,4,2048]{4,3,2,1,0:T(4,128)(2,1)} %constant_dynamic-update-slice_fusion.8, bf16[1,2,64,2048]{3,2,1,0:T(8,128)(2,1)} %param.5), kind=kLoop, calls=%fused_computation.29 | loop fusion | bytes 65536
  13.2 1.5 %constant_dynamic-update-slice_fusion.6 = bf16[16,1,2,4,2048]{4,3,2,1,0:T(4,128)(2,1)} fusion(bf16[16,1,2,4,2048]{4,3,2,1,0:T(4,128)(2,1)} %constant_dynamic-update-slice_fusion.7, bf16[1,2,64,2048]{3,2,1,0:T(8,128)(2,1)} %param.5), kind=kLoop, calls=%fused_computation.28 | loop fusion | bytes 65536
  14.7 1.5 %constant_dynamic-update-slice_fusion.5 = bf16[16,1,2,4,2048]{4,3,2,1,0:T(4,128)(2,1)} fusion(bf16[16,1,2,4,2048]{4,3,2,1,0:T(4,128)(2,1)} %constant_dynamic-update-slice_fusion.6, bf16[1,2,64,2048]{3,2,1,0:T(8,128)(2,1)} %param.5), kind=kLoop, calls=%fused_computation.27 | loop fusion | bytes 65536
  16.1 1.5 %constant_dynamic-update-slice_fusion.4 = bf16[16,1,2,4,2048]{4,3,2,1,0:T(4,128)(2,1)} fusion(bf16[16,1,2,4,2048]{4,3,2,1,0:T(4,128)(2,1)} %constant_dynamic-update-slice_fusion.5, bf16[1,2,64,2048]{3,2,1,0:T(8,128)(2,1)} %param.5), kind=kLoop, calls=%fused_computation.26 | loop fusion | bytes 65536
  17.6 1.5 %constant_dynamic-update-slice_fusion.3 = bf16[16,1,2,4,2048]{4,3,2,1,0:T(4,128)(2,1)} fusion(bf16[16,1,2,4,2048]{4,3,2,1,0:T(4,128)(2,1)} %constant_dynamic-update-slice_fusion.4, bf16[1,2,64,2048]{3,2,1,0:T(8,128)(2,1)} %param.5), kind=kLoop, calls=%fused_computation.25 | loop fusion | bytes 65536
  19.1 1.5 %constant_dynamic-update-slice_fusion.2 = bf16[16,1,2,4,2048]{4,3,2,1,0:T(4,128)(2,1)} fusion(bf16[16,1,2,4,2048]{4,3,2,1,0:T(4,128)(2,1)} %constant_dynamic-update-slice_fusion.3, bf16[1,2,64,2048]{3,2,1,0:T(8,128)(2,1)} %param.5), kind=kLoop, calls=%fused_computation.24 | loop fusion | bytes 65536
  20.5 1.5 %constant_dynamic-update-slice_fusion.1 = bf16[16,1,2,4,2048]{4,3,2,1,0:T(4,128)(2,1)} fusion(bf16[16,1,2,4,2048]{4,3,2,1,0:T(4,128)(2,1)} %constant_dynamic-update-slice_fusion.2, bf16[1,2,64,2048]{3,2,1,0:T(8,128)(2,1)} %param.5), kind=kLoop, calls=%fused_computation.23 | loop fusion | bytes 65536
  22.0 1.5 %constant_dynamic-update-slice_fusion = bf16[16,1,2,4,2048]{4,3,2,1,0:T(4,128)(2,1)} fusion(bf16[16,1,2,4,2048]{4,3,2,1,0:T(4,128)(2,1)} %constant_dynamic-update-slice_fusion.1, bf16[1,2,64,2048]{3,2,1,0:T(8,128)(2,1)} %param.5), kind=kLoop, calls=%fused_computation.22 | loop fusion | bytes 65536 | tf_op jit(solution)/shard_map/stack | solution.py:34
  23.5 7.4 %all-to-all-start = ((bf16[16,1,2,4,2048]{4,3,2,1,0:T(4,128)(2,1)}), bf16[16,1,2,4,2048]{4,3,2,1,0:T(4,128)(2,1)S(1)}, u32[]{:S(2)}, u32[]{:S(2)}) async-start(bf16[16,1,2,4,2048]{4,3,2,1,0:T(4,128)(2,1)} %constant_dynamic-update-slice_fusion), calls=%async_computation | async-start | bytes 1048576 | tf_op jit(solution)/shard_map/all_to_all | solution.py:35
  30.9 0.0 copy-done.1
  30.9 14.2 %all-to-all-done = bf16[16,1,2,4,2048]{4,3,2,1,0:T(4,128)(2,1)S(1)} async-done(((bf16[16,1,2,4,2048]{4,3,2,1,0:T(4,128)(2,1)}), bf16[16,1,2,4,2048]{4,3,2,1,0:T(4,128)(2,1)S(1)}, u32[]{:S(2)}, u32[]{:S(2)}) %all-to-all-start) | async-done | bytes 524320 | tf_op jit(solution)/shard_map/all_to_all | solution.py:35
  45.2 2.4 %gather_fusion = bf16[64,2,4,2048]{3,2,1,0:T(4,128)(2,1)S(1)} fusion(bf16[16,2,4,2048]{3,2,1,0:T(4,128)(2,1)S(1)} %bitcast.57, s32[1024]{0:T(1024)S(1)} %pad_clamp_fusion.1), kind=kCustom, calls=%fused_computation.clone | custom fusion | bytes 4194560 | tf_op jit(solution)/shard_map/jit(_take)/gather | solution.py:37
  47.5 3.6 %gather_fusion.1 = bf16[64,2,4,2048]{3,2,1,0:T(4,128)(2,1)} fusion(bf16[16,2,4,2048]{3,2,1,0:T(4,128)(2,1)S(1)} %bitcast.58, s32[1024]{0:T(1024)S(1)} %pad_clamp_fusion), kind=kCustom, calls=%fused_computation.1.clone | custom fusion | bytes 4194560 | tf_op jit(solution)/shard_map/jit(_take)/gather | solution.py:38
  51.1 7.5 %fusion = (f32[64,2,4,2048]{3,0,2,1:T(8,128)S(1)}, f32[64,2,4,2048]{3,0,2,1:T(8,128)S(1)}) fusion(bf16[64,2,4,2048]{3,2,1,0:T(4,128)(2,1)} %gather_fusion.1, pred[64]{0:T(512)(128)(4,1)S(1)} %get-tuple-element.13, bf16[64,2,4,2048]{3,2,1,0:T(4,128)(2,1)S(1)} %gather_fusion, pred[64]{0:T(512)(128)(4,1)S(1)} %get-tuple-element.6), kind=kLoop, calls=%fused_computation.4 | loop fusion | flops 4194304 | bytes 12583040 | tf_op jit(solution)/shard_map/convert_element_type | solution.py:12
  58.6 1.6 %subtract_bitcast_fusion = (f32[1,64,4,2048]{3,1,2,0:T(8,128)S(1)}, f32[1,64,4,2048]{3,1,2,0:T(8,128)S(1)}, f32[1,64,4,2048]{3,1,2,0:T(8,128)S(1)}) fusion(f32[64,2,4,2048]{3,0,2,1:T(8,128)S(1)} %get-tuple-element.15, f32[64,2,4,2048]{3,0,2,1:T(8,128)S(1)} %get-tuple-element.16), kind=kLoop, calls=%fused_computation.9 | loop fusion | flops 4718592 | bytes 14680064 | tf_op jit(solution)/shard_map/sub | solution.py:13
  60.2 0.7 %maximum_reduce_fusion = f32[3,64,2048]{2,1,0:T(8,128)S(1)} fusion(f32[1,64,4,2048]{3,1,2,0:T(8,128)S(1)} %get-tuple-element.12, f32[1,64,4,2048]{3,1,2,0:T(8,128)S(1)} %get-tuple-element.11, f32[1,64,4,2048]{3,1,2,0:T(8,128)S(1)} %get-tuple-element.10), kind=kLoop, calls=%fused_computation.2 | loop fusion | flops 4325376 | bytes 7864320 | tf_op jit(solution)/shard_map/reduce_sum | solution.py:18
  60.9 1.0 %fusion.3 = f32[3,64,128]{2,1,0:T(8,128)S(1)} fusion(f32[3,64,2048]{2,1,0:T(8,128)S(1)} %maximum_reduce_fusion, s32[2048]{0:T(1024)S(1)} %add_select_fusion), kind=kOutput, calls=%fused_computation.13 | convolution fusion | flops 604241920 | bytes 1679360 | tf_op jit(solution)/shard_map/dot_general | solution.py:22
  61.9 0.0 copy-done
  61.9 0.1 convolution_bitcast_fusion
  62.1 0.6 copy.24
  (4 shorter events, 0.0 us)
Async XLA Ops:
  0.0 61.9 %copy-start = (bf16[15,64]{1,0:T(8,128)(2,1)S(1)}, bf16[15,64]{1,0:T(8,128)(2,1)}, u32[]{:S(2)}) copy-start(bf16[15,64]{1,0:T(8,128)(2,1)} %param.7) | copy-start | bytes 5764
  0.0 30.9 %copy-start.1 = (s32[64,2]{0,1:T(2,128)S(1)}, s32[64,2]{0,1:T(2,128)}, u32[]{:S(2)}) copy-start(s32[64,2]{0,1:T(2,128)} %param.6) | copy-start | bytes 1540
  23.5 21.7 %all-to-all-start = ((bf16[16,1,2,4,2048]{4,3,2,1,0:T(4,128)(2,1)}), bf16[16,1,2,4,2048]{4,3,2,1,0:T(4,128)(2,1)S(1)}, u32[]{:S(2)}, u32[]{:S(2)}) async-start(bf16[16,1,2,4,2048]{4,3,2,1,0:T(4,128)(2,1)} %constant_dynamic-update-slice_fusion), calls=%async_computation | async-start | bytes 1048576 | tf_op jit(solution)/shard_map/all_to_all | solution.py:35
